TPU v7x, 128 devices: a whole 4x4x4 slice. The times are simulated.
128 devices in a mesh: expert: 16 (over z, x), dp: 8 (over y, core).
Axes of the slice: x: 4, y: 4, z: 4, core: 2. Of those that a mesh axis runs over, the one named last changes fastest.
Arguments:
- tokens: bfloat16 [16, 480, 7168], P('expert', 'dp'), may hold values from -6 to 6
- cotangent: bfloat16 [16, 480, 7168], P('expert', 'dp'), may hold values from -1.5 to 1.5
- counts: int32 [16, 8], replicated, may hold values from 1 to 60, as said below
- w_gate: bfloat16 [16, 7168, 2048], P('expert', None, 'dp'), may hold values from -0.0625 to 0.0625
- w_up: bfloat16 [16, 7168, 2048], P('expert', None, 'dp'), may hold values from -0.0625 to 0.0625
- w_down: bfloat16 [16, 2048, 7168], P('expert', 'dp'), may hold values from -0.125 to 0.125
Outputs:
- outputs: bfloat16 [16, 480, 7168], P('expert', 'dp')
- input_grads: bfloat16 [16, 480, 7168], P('expert', 'dp')
- gate_grad: bfloat16 [16, 7168, 2048], P('expert', None, 'dp')
- up_grad: bfloat16 [16, 7168, 2048], P('expert', None, 'dp')
- down_grad: bfloat16 [16, 2048, 7168], P('expert', 'dp')
Inputs may be any that keep to these rules, and one draw needn't show every extreme that they name: For each expert e below 8, exactly one of experts e and e + 8 is hot: all its counts exceed 40 - 20 and one equals 60; every count of the other is at most 20 and one equals 20.
All inputs are finite; a program needn't handle non-finite values.
Results may differ from a plain program's by a relative error of at most 0.012.
Values may be sent and summed in bfloat16 or wider, within the bound.
No kernel may reach another device: no remote copies, remote signals or barrier semaphores. Data moves between devices by JAX's collectives and lax.ppermute only.
A program may use at most 192 MiB of HBM per device.

v0:
```python
import jax
import jax.numpy as jnp
from jax import lax
from jax.sharding import PartitionSpec as P


def silu_slope(value):
    sigma = jax.nn.sigmoid(value)
    return sigma * (1.0 + value * (1.0 - sigma))


def contract_last(left, right):
    return lax.dot_general(
        left, right, (((1,), (1,)), ((), ())), preferred_element_type=jnp.float32
    )


def contract_first(left, right):
    return lax.dot_general(
        left, right, (((0,), (0,)), ((), ())), preferred_element_type=jnp.float32
    )


def expert_work(rows, cot_rows, gate_w, up_w, down_w):
    gate = jnp.dot(rows, gate_w, preferred_element_type=jnp.float32)
    up = jnp.dot(rows, up_w, preferred_element_type=jnp.float32)
    active = jax.nn.silu(gate)
    hidden = (active * up).astype(jnp.bfloat16)
    out_part = jnp.dot(hidden, down_w, preferred_element_type=jnp.float32).astype(jnp.bfloat16)
    out_part, hidden, gate, up = lax.optimization_barrier((out_part, hidden, gate, up))
    active = jax.nn.silu(gate)
    hidden_grad = contract_last(cot_rows, down_w)
    gate_act = (hidden_grad * up * silu_slope(gate)).astype(jnp.bfloat16)
    up_act = (hidden_grad * active).astype(jnp.bfloat16)
    in_part = contract_last(gate_act, gate_w) + contract_last(up_act, up_w)
    gate_term = contract_first(rows, gate_act)
    up_term = contract_first(rows, up_act)
    down_term = contract_first(hidden, cot_rows)
    return (out_part, in_part, gate_term, up_term, down_term)


def shards(tokens, cotangent, counts, w_gate, w_up, w_down):
    rows_in = tokens[0]
    cot_in = cotangent[0]
    gate_w = w_gate[0]
    up_w = w_up[0]
    down_w = w_down[0]
    expert_pos = lax.axis_index("expert")
    batch_pos = lax.axis_index("dp")
    expert_ids = jnp.arange(counts.shape[0], dtype=jnp.int32)
    batch_ids = jnp.arange(counts.shape[1], dtype=jnp.int32)
    own_counts = jnp.sum(jnp.where(expert_ids[:, None] == expert_pos, counts, 0), axis=0)
    own_total = jnp.sum(jnp.where(batch_ids == batch_pos, own_counts, 0))
    slots = rows_in.shape[0]
    valid = (jnp.arange(slots, dtype=jnp.int32) < own_total)[:, None]
    masked = jnp.where(valid, rows_in, jnp.zeros_like(rows_in))
    masked_cot = jnp.where(valid, cot_in, jnp.zeros_like(cot_in))
    all_rows = lax.all_gather(masked, "dp", axis=0, tiled=True)
    all_cot = lax.all_gather(masked_cot, "dp", axis=0, tiled=True)
    out_part, in_part, gate_term, up_term, down_term = expert_work(
        all_rows, all_cot, gate_w, up_w, down_w
    )
    groups = lax.axis_size("dp")
    outputs = lax.psum_scatter(
        out_part.reshape(groups, slots, -1), "dp", scatter_dimension=0, tiled=False
    )
    input_grads = lax.psum_scatter(
        in_part.astype(jnp.bfloat16).reshape(groups, slots, -1),
        "dp",
        scatter_dimension=0,
        tiled=False,
    )
    gate_grad = gate_term.astype(jnp.bfloat16)
    up_grad = up_term.astype(jnp.bfloat16)
    down_grad = down_term.astype(jnp.bfloat16)
    return (outputs[None], input_grads[None], gate_grad[None], up_grad[None], down_grad[None])


def solution(mesh):
    placed = (
        P("expert", "dp", None),
        P("expert", "dp", None),
        P(),
        P("expert", None, "dp"),
        P("expert", None, "dp"),
        P("expert", "dp", None),
    )
    return jax.shard_map(
        shards,
        mesh=mesh,
        in_specs=placed,
        out_specs=(
            P("expert", "dp", None),
            P("expert", "dp", None),
            P("expert", None, "dp"),
            P("expert", None, "dp"),
            P("expert", "dp", None),
        ),
        check_vma=False,
    )
```

profile of v0, /device:TPU:1, one launch (start us, length us, event | category | flops | bytes accessed | tf_op | source)
XLA Modules:
  0.0 215.1 jit_solution(16203403560469040614)
XLA Ops:
  7.2 0.0 all-gather.5.cloned.1.call-start
  7.2 0.8 select_reduce_fusion
  8.0 0.6 fusion.15
  8.7 0.6 iota_compare_fusion.1
  9.3 2.9 %fusion.13 = (bf16[1,60,7168]{2,1,0:T(8,128)(2,1)}, bf16[1,60,7168]{2,1,0:T(8,128)(2,1)}) fusion(bf16[1,60,7168]{2,1,0:T(8,128)(2,1)} %param.7, pred[60]{0:T(512)(128)(4,1)S(1)} %iota_compare_fusion.1, bf16[1,60,7168]{2,1,0:T(8,128)(2,1)} %param.6), kind=kLoop, calls=%fused_computation.19 | loop fusion | flops 860160 | bytes 3440700
  12.2 0.0 all-gather.5.cloned.1.call-update
  12.2 0.0 all-gather.7.cloned.1.call-start
  12.3 0.7 all-gather.7.cloned.1.call-update
  13.0 0.0 reduce-scatter.3.cloned.1.call-start
  13.0 48.2 %all-gather.5.cloned.1.call-done = bf16[8,60,7168]{2,1,0:T(8,128)(2,1)} async-done(((bf16[1,60,7168]{2,1,0:T(8,128)(2,1)}), bf16[8,60,7168]{2,1,0:T(8,128)(2,1)}) %all-gather.5.cloned.1.call-update) | async-done | bytes 6881296 | tf_op jit(solution)/shard_map/all_gather | solution.py:58
  61.3 6.9 %reshape.28 = bf16[480,7168]{1,0:T(8,128)(2,1)} reshape(bf16[8,60,7168]{2,1,0:T(8,128)(2,1)} %all-gather.5.cloned.1.call-done) | data formatting | bytes 13762560
  68.2 0.0 copy-start
  68.2 0.0 copy-start.1
  68.2 6.2 %fusion.11 = f32[480,256]{1,0:T(8,128)S(1)} fusion(bf16[480,7168]{1,0:T(8,128)(2,1)} %reshape.28, bf16[1,7168,256]{2,1,0:T(8,128)(2,1)} %param.9), kind=kOutput, calls=%fused_computation.16 | convolution fusion | flops 1761607680 | bytes 11042816 | tf_op jit(solution)/shard_map/dot_general | solution.py:25
  74.3 0.4 copy-done
  74.8 1.6 copy-done.1
  76.4 0.0 copy-start.3
  76.4 1.9 multiply_convert_fusion.2
  78.4 0.1 copy-done.3
  78.4 4.8 %convolution_convert_fusion = bf16[480,7168]{1,0:T(8,128)(2,1)} fusion(bf16[480,256]{1,0:T(8,128)(2,1)S(1)} %get-tuple-element.12, bf16[1,256,7168]{2,1,0:T(8,128)(2,1)S(1)} %copy-done.3), kind=kOutput, calls=%fused_computation.1 | convolution fusion | flops 1765048320 | bytes 10797056 | tf_op jit(solution)/shard_map/dot_general | solution.py:29
  83.2 6.9 %reshape.25 = bf16[8,60,7168]{2,1,0:T(8,128)(2,1)} reshape(bf16[480,7168]{1,0:T(8,128)(2,1)} %convolution_convert_fusion) | data formatting | bytes 13762560 | tf_op jit(solution)/shard_map/reshape | solution.py:65
  90.1 0.0 reduce-scatter.3.cloned.1.call-update
  90.2 0.2 reduce-scatter.5.cloned.1.call-start
  90.4 18.5 %all-gather.7.cloned.1.call-done = bf16[8,60,7168]{2,1,0:T(8,128)(2,1)} async-done(((bf16[1,60,7168]{2,1,0:T(8,128)(2,1)}), bf16[8,60,7168]{2,1,0:T(8,128)(2,1)}) %all-gather.7.cloned.1.call-update) | async-done | bytes 6881296 | tf_op jit(solution)/shard_map/all_gather | solution.py:59
  108.9 6.8 %reshape.30 = bf16[480,7168]{1,0:T(8,128)(2,1)} reshape(bf16[8,60,7168]{2,1,0:T(8,128)(2,1)} %all-gather.7.cloned.1.call-done) | data formatting | bytes 13762560
  115.7 0.0 copy-start.4
  115.7 6.2 %multiply_convert_fusion = (bf16[480,256]{1,0:T(8,128)(2,1)S(1)}, bf16[480,256]{1,0:T(8,128)(2,1)S(1)}) fusion(f32[480,256]{1,0:T(8,128)S(1)} %fusion.11, f32[480,256]{1,0:T(8,128)S(1)} %get-tuple-element.10, bf16[480,7168]{1,0:T(8,128)(2,1)} %reshape.30, bf16[1,256,7168]{2,1,0:T(8,128)(2,1)} %param.11), kind=kOutput, calls=%fused_computation.22 | convolution fusion | flops 1763205120 | bytes 12025856 | tf_op jit(solution)/shard_map/dot_general | solution.py:13
  121.9 0.0 copy-done.4
  121.9 0.0 copy-start.2
  121.9 6.9 %fusion.9 = f32[480,7168]{1,0:T(8,128)} fusion(bf16[480,256]{1,0:T(8,128)(2,1)S(1)} %get-tuple-element.14, bf16[1,7168,256]{2,1,0:T(8,128)(2,1)S(1)} %copy-done.4), kind=kOutput, calls=%fused_computation.14 | convolution fusion | flops 1761607680 | bytes 17678336 | tf_op jit(solution)/shard_map/dot_general | solution.py:13
  128.8 0.0 copy-done.2
  128.8 10.0 %add_convert_fusion = bf16[480,7168]{1,0:T(8,128)(2,1)} fusion(f32[480,7168]{1,0:T(8,128)} %fusion.9, bf16[480,256]{1,0:T(8,128)(2,1)S(1)} %get-tuple-element.13, bf16[1,7168,256]{2,1,0:T(8,128)(2,1)S(1)} %copy-done.2), kind=kOutput, calls=%fused_computation | convolution fusion | flops 1768488960 | bytes 24559616 | tf_op jit(solution)/shard_map/dot_general | solution.py:13
  138.9 7.0 %reshape.26 = bf16[8,60,7168]{2,1,0:T(8,128)(2,1)} reshape(bf16[480,7168]{1,0:T(8,128)(2,1)} %add_convert_fusion) | data formatting | bytes 13762560 | tf_op jit(solution)/shard_map/reshape | solution.py:68
  145.8 0.0 slice-start
  145.8 0.0 reduce-scatter.5.cloned.1.call-update
  145.9 0.0 slice-start.1
  145.9 7.2 %fusion.2 = bf16[1,256,7168]{2,1,0:T(8,128)(2,1)} fusion(bf16[480,256]{1,0:T(8,128)(2,1)S(1)} %get-tuple-element.12, bf16[480,7168]{1,0:T(8,128)(2,1)} %reshape.30), kind=kOutput, calls=%fused_computation.7 | convolution fusion | flops 1763442688 | bytes 10797056 | tf_op jit(solution)/shard_map/dot_general | solution.py:19
  153.1 0.0 slice-done
  153.1 0.0 slice-done.1
  153.1 4.0 %fusion.1 = bf16[1,7168,256]{2,1,0:T(8,128)(2,1)} fusion(bf16[480,7168]{1,0:T(8,128)(2,1)S(1)} %bitcast.50, bf16[480,256]{1,0:T(8,128)(2,1)S(1)} %get-tuple-element.13), kind=kOutput, calls=%fused_computation.6 | convolution fusion | flops 1763442688 | bytes 10797056 | tf_op jit(solution)/shard_map/dot_general | solution.py:19
  157.1 4.0 %fusion = bf16[1,7168,256]{2,1,0:T(8,128)(2,1)} fusion(bf16[480,7168]{1,0:T(8,128)(2,1)S(1)} %bitcast.50, bf16[480,256]{1,0:T(8,128)(2,1)S(1)} %get-tuple-element.14), kind=kOutput, calls=%fused_computation.5 | convolution fusion | flops 1763442688 | bytes 10797056 | tf_op jit(solution)/shard_map/dot_general | solution.py:19
  161.1 0.0 reduce-scatter.3.cloned.1.call-done
  161.1 47.4 %reduce-scatter.5.cloned.1.call-done = bf16[1,60,7168]{2,1,0:T(8,128)(2,1)} async-done(((bf16[8,60,7168]{2,1,0:T(8,128)(2,1)}), bf16[1,60,7168]{2,1,0:T(8,128)(2,1)}) %reduce-scatter.5.cloned.1.call-update) | async-done | bytes 860176 | tf_op jit(solution)/shard_map/reduce_scatter | solution.py:67
  (2 shorter events, 0.0 us)
Async XLA Ops:
  7.2 54.1 %all-gather.5.cloned.1.call-start = ((), (), s32[]{:S(2)}) async-start(), calls=%async_computation.4 | async-start | bytes 8257536 | tf_op jit(solution)/shard_map/all_gather | solution.py:58
  12.2 96.7 %all-gather.7.cloned.1.call-start = ((), (), s32[]{:S(2)}) async-start(), calls=%async_computation.5 | async-start | bytes 8257536 | tf_op jit(solution)/shard_map/all_gather | solution.py:59
  13.0 148.2 %reduce-scatter.3.cloned.1.call-start = ((), (), s32[]{:S(2)}) async-start(), calls=%async_computation.2 | async-start | bytes 8257536 | tf_op jit(solution)/shard_map/reduce_scatter | solution.py:64
  68.2 6.6 %copy-start = (bf16[480,7168]{1,0:T(8,128)(2,1)S(1)}, bf16[480,7168]{1,0:T(8,128)(2,1)}, u32[]{:S(2)}) copy-start(bf16[480,7168]{1,0:T(8,128)(2,1)} %reshape.28) | copy-start | bytes 20643844
  68.2 8.2 %copy-start.1 = (bf16[1,7168,256]{2,1,0:T(8,128)(2,1)S(1)}, bf16[1,7168,256]{2,1,0:T(8,128)(2,1)}, u32[]{:S(2)}) copy-start(bf16[1,7168,256]{2,1,0:T(8,128)(2,1)} %param.10) | copy-start | bytes 11010052
  76.4 2.0 copy-start.3
  90.2 118.4 %reduce-scatter.5.cloned.1.call-start = ((), (), s32[]{:S(2)}) async-start(), calls=%async_computation.3 | async-start | bytes 8257536 | tf_op jit(solution)/shard_map/reduce_scatter | solution.py:67
  115.7 6.2 %copy-start.4 = (bf16[1,7168,256]{2,1,0:T(8,128)(2,1)S(1)}, bf16[1,7168,256]{2,1,0:T(8,128)(2,1)}, u32[]{:S(2)}) copy-start(bf16[1,7168,256]{2,1,0:T(8,128)(2,1)} %param.9) | copy-start | bytes 11010052
  121.9 7.0 %copy-start.2 = (bf16[1,7168,256]{2,1,0:T(8,128)(2,1)S(1)}, bf16[1,7168,256]{2,1,0:T(8,128)(2,1)}, u32[]{:S(2)}) copy-start(bf16[1,7168,256]{2,1,0:T(8,128)(2,1)} %param.10) | copy-start | bytes 11010052
  145.8 7.2 %slice-start = ((s8[6881280]{0:T(1024)(128)(4,1)}), s8[2686976]{0:T(1024)(128)(4,1)S(1)}, s32[]{:S(2)}) async-start(s8[6881280]{0:T(1024)(128)(4,1)} %bitcast.49), calls=%async_computation.6 | async-start | bytes 5373952
  145.9 7.2 %slice-start.1 = ((s8[6881280]{0:T(1024)(128)(4,1)}), s8[4194304]{0:T(1024)(128)(4,1)S(1)}, s32[]{:S(2)}) async-start(s8[6881280]{0:T(1024)(128)(4,1)} %bitcast.49), calls=%async_computation.7 | async-start | bytes 8388608
Sparse Core Ops, SparseCore 0:
  12.3 48.8 all-gather.4
  63.5 45.3 all-gather.6
  111.9 46.6 reduce-scatter.2
  161.4 47.0 reduce-scatter.4
where the time goes:
time: 215 us
  waiting for transfers between devices  115 us (53%)
  matrix products  51.3 us (24%)
  local copies, waits for them, and re-layouts  29.7 us (14%)
  between operations  13.8 us (6%)
  other arithmetic  4.97 us (2%)
    all_gather x1, waiting for transfers between devices, shards(): all_rows = lax.all_gather(masked, 'dp', axis=0, tiled=True)  48.2 us
    reduce_scatter x1, waiting for transfers between devices, shards(): lax.psum_scatter(in_part.astype(jnp.bfloat16).reshape(groups, slots, -1),...  47.4 us
    dot_general x3, matrix products, contract_last(): lax.dot_general(left, right, (((1,), (1,)), ((), ())), preferred_element_...  23.2 us
    all_gather x1, waiting for transfers between devices, shards(): all_cot = lax.all_gather(masked_cot, 'dp', axis=0, tiled=True)  18.5 us
    unnamed x16, local copies, waits for them, and re-layouts  15.9 us
    dot_general x3, matrix products, contract_first(): lax.dot_general(left, right, (((0,), (0,)), ((), ())), preferred_element_...  15.2 us
    reshape x1, local copies, waits for them, and re-layouts, shards(): in_part.astype(jnp.bfloat16).reshape(groups, slots, -1)  6.95 us
    reshape x1, local copies, waits for them, and re-layouts, shards(): out_part.reshape(groups, slots, -1)  6.9 us
  transfers between devices with their start and end apart: 4, of which 3 were waited for; matrix products, arithmetic and copies ran while one was open for 37% of the time, Pallas kernels for 0%

commit v1 on v0

--- a/solution.py
+++ b/solution.py
@@ -56,7 +56,10 @@
     masked = jnp.where(valid, rows_in, jnp.zeros_like(rows_in))
     masked_cot = jnp.where(valid, cot_in, jnp.zeros_like(cot_in))
     all_rows = lax.all_gather(masked, "dp", axis=0, tiled=True)
-    all_cot = lax.all_gather(masked_cot, "dp", axis=0, tiled=True)
+    n_dev = lax.axis_size("dp")
+    blocks = jnp.stack([masked_cot for _ in range(n_dev)])
+    blocks = lax.all_to_all(blocks, "dp", split_axis=0, concat_axis=0)
+    all_cot = jnp.concatenate(blocks, axis=0)
     out_part, in_part, gate_term, up_term, down_term = expert_work(
         all_rows, all_cot, gate_w, up_w, down_w
     )

time: 215 us -> 301 us (1.40)
  blocking collectives: 0 us -> 120 us
  waiting for transfers between devices: 115 us -> 80.6 us
    all_to_all x0 -> x1, blocking collectives: none -> 120 us  [shards(): blocks = lax.all_to_all(blocks, 'dp', split_axis=0, concat_axis=0)]
    all_gather x1 -> x0, waiting for transfers between devices: 18.5 us -> none  [shards(): all_cot = lax.all_gather(masked_cot, 'dp', axis=0, tiled=True)]
    reduce_scatter x1, waiting for transfers between devices: 47.4 us -> 31.6 us  [shards(): lax.psum_scatter(in_part.astype(jnp.bfloat16).reshape(groups, slots, -1),...]
    unnamed x16 -> x17, local copies, waits for them, and re-layouts: 15.9 us -> 9.04 us
    reshape x0 -> x1, local copies, waits for them, and re-layouts: none -> 6.82 us  [shards(): all_cot = jnp.concatenate(blocks, axis=0)]
  transfers between devices with their start and end apart: 4 -> 3, of which waited for: 3 -> 2; matrix products, arithmetic and copies ran while one was open for 37% -> 17% of each run, Pallas kernels for 0% -> 0%
where the time goes in v1:
time: 301 us
  blocking collectives  120 us (40%)
  waiting for transfers between devices  80.6 us (27%)
  matrix products  50.8 us (17%)
  local copies, waits for them, and re-layouts  30.4 us (10%)
  between operations  13.8 us (5%)
  other arithmetic  4.46 us (1%)
    all_to_all x1, blocking collectives, shards(): blocks = lax.all_to_all(blocks, 'dp', split_axis=0, concat_axis=0)  120 us
    all_gather x1, waiting for transfers between devices, shards(): all_rows = lax.all_gather(masked, 'dp', axis=0, tiled=True)  49 us
    reduce_scatter x1, waiting for transfers between devices, shards(): lax.psum_scatter(in_part.astype(jnp.bfloat16).reshape(groups, slots, -1),...  31.6 us
    dot_general x3, matrix products, contract_last(): lax.dot_general(left, right, (((1,), (1,)), ((), ())), preferred_element_...  22.8 us
    dot_general x3, matrix products, contract_first(): lax.dot_general(left, right, (((0,), (0,)), ((), ())), preferred_element_...  15.1 us
    unnamed x17, local copies, waits for them, and re-layouts  9.04 us
    reshape x1, local copies, waits for them, and re-layouts, shards(): in_part.astype(jnp.bfloat16).reshape(groups, slots, -1)  6.83 us
    reshape x1, local copies, waits for them, and re-layouts, shards(): all_cot = jnp.concatenate(blocks, axis=0)  6.82 us
  transfers between devices with their start and end apart: 3, of which 2 were waited for; matrix products, arithmetic and copies ran while one was open for 17% of the time, Pallas kernels for 0%

profile of v1, /device:TPU:1, one launch (start us, length us, event | category | flops | bytes accessed | tf_op | source)
XLA Modules:
  0.0 300.6 jit_solution(17052125042239862696)
XLA Ops:
  7.2 0.0 all-gather.3.cloned.1.call-start
  7.2 0.8 select_reduce_fusion
  8.0 0.6 fusion.14
  8.7 0.6 iota_compare_fusion.1
  9.3 2.2 fusion.13
  11.6 0.0 all-gather.3.cloned.1.call-update
  11.6 0.0 reduce-scatter.3.cloned.1.call-start
  11.6 49.0 %all-gather.3.cloned.1.call-done = bf16[8,60,7168]{2,1,0:T(8,128)(2,1)} async-done(((bf16[1,60,7168]{2,1,0:T(8,128)(2,1)}), bf16[8,60,7168]{2,1,0:T(8,128)(2,1)}) %all-gather.3.cloned.1.call-update) | async-done | bytes 6881296 | tf_op jit(solution)/shard_map/all_gather | solution.py:58
  60.6 6.9 %reshape.40 = bf16[480,7168]{1,0:T(8,128)(2,1)} reshape(bf16[8,60,7168]{2,1,0:T(8,128)(2,1)} %all-gather.3.cloned.1.call-done) | data formatting | bytes 13762560
  67.5 0.0 copy-start
  67.5 0.0 copy-start.1
  67.5 6.1 %fusion.11 = f32[480,256]{1,0:T(8,128)S(1)} fusion(bf16[480,7168]{1,0:T(8,128)(2,1)} %reshape.40, bf16[1,7168,256]{2,1,0:T(8,128)(2,1)} %param.9), kind=kOutput, calls=%fused_computation.16 | convolution fusion | flops 1761607680 | bytes 11042816 | tf_op jit(solution)/shard_map/dot_general | solution.py:25
  73.6 0.0 copy-done
  73.6 0.9 copy-done.1
  74.5 0.0 copy-start.3
  74.5 1.9 multiply_convert_fusion.2
  76.5 0.1 copy-done.3
  76.6 4.8 %convolution_convert_fusion = bf16[480,7168]{1,0:T(8,128)(2,1)} fusion(bf16[480,256]{1,0:T(8,128)(2,1)S(1)} %get-tuple-element.12, bf16[1,256,7168]{2,1,0:T(8,128)(2,1)S(1)} %copy-done.3), kind=kOutput, calls=%fused_computation.1 | convolution fusion | flops 1765048320 | bytes 10797056 | tf_op jit(solution)/shard_map/dot_general | solution.py:29
  81.4 6.8 %reshape.36 = bf16[8,60,7168]{2,1,0:T(8,128)(2,1)} reshape(bf16[480,7168]{1,0:T(8,128)(2,1)} %convolution_convert_fusion) | data formatting | bytes 13762560 | tf_op jit(solution)/shard_map/reshape | solution.py:68
  88.2 0.0 copy-start.5
  88.2 0.0 reduce-scatter.3.cloned.1.call-update
  88.2 0.0 reduce-scatter.5.cloned.1.call-start
  88.3 1.1 copy-done.5
  89.4 0.1 select_bitcast_fusion
  89.5 0.9 stack.5
  90.4 120.4 %all_to_all.5 = bf16[8,60,7168]{2,1,0:T(8,128)(2,1)} all-to-all(bf16[8,60,7168]{2,1,0:T(8,128)(2,1)S(1)} %stack.5), channel_id=1, replica_groups=mesh['expert'=16,'dp'=8] {'dp'}, dimensions={0} | all-to-all | bytes 13762560 | tf_op jit(solution)/shard_map/all_to_all | solution.py:61
  210.8 6.8 %reshape.37 = bf16[480,7168]{1,0:T(8,128)(2,1)} reshape(bf16[8,60,7168]{2,1,0:T(8,128)(2,1)} %all_to_all.5) | data formatting | bytes 13762560 | tf_op jit(solution)/shard_map/reshape | solution.py:62
  217.6 0.0 copy-start.4
  217.6 6.2 %multiply_convert_fusion = (bf16[480,256]{1,0:T(8,128)(2,1)S(1)}, bf16[480,256]{1,0:T(8,128)(2,1)S(1)}) fusion(f32[480,256]{1,0:T(8,128)S(1)} %fusion.11, f32[480,256]{1,0:T(8,128)S(1)} %get-tuple-element.10, bf16[480,7168]{1,0:T(8,128)(2,1)} %reshape.37, bf16[1,256,7168]{2,1,0:T(8,128)(2,1)} %param.11), kind=kOutput, calls=%fused_computation.21 | convolution fusion | flops 1763205120 | bytes 12025856 | tf_op jit(solution)/shard_map/dot_general | solution.py:13
  223.8 0.0 copy-done.4
  223.8 0.0 copy-start.2
  223.8 6.9 %fusion.9 = f32[480,7168]{1,0:T(8,128)} fusion(bf16[480,256]{1,0:T(8,128)(2,1)S(1)} %get-tuple-element.14, bf16[1,7168,256]{2,1,0:T(8,128)(2,1)S(1)} %copy-done.4), kind=kOutput, calls=%fused_computation.14 | convolution fusion | flops 1761607680 | bytes 17678336 | tf_op jit(solution)/shard_map/dot_general | solution.py:13
  230.7 0.0 copy-done.2
  230.8 9.7 %add_convert_fusion = bf16[480,7168]{1,0:T(8,128)(2,1)} fusion(f32[480,7168]{1,0:T(8,128)} %fusion.9, bf16[480,256]{1,0:T(8,128)(2,1)S(1)} %get-tuple-element.13, bf16[1,7168,256]{2,1,0:T(8,128)(2,1)S(1)} %copy-done.2), kind=kOutput, calls=%fused_computation | convolution fusion | flops 1768488960 | bytes 24559616 | tf_op jit(solution)/shard_map/dot_general | solution.py:13
  240.5 6.8 %reshape.38 = bf16[8,60,7168]{2,1,0:T(8,128)(2,1)} reshape(bf16[480,7168]{1,0:T(8,128)(2,1)} %add_convert_fusion) | data formatting | bytes 13762560 | tf_op jit(solution)/shard_map/reshape | solution.py:71
  247.3 0.0 slice-start
  247.3 0.0 reduce-scatter.5.cloned.1.call-update
  247.3 0.0 slice-start.1
  247.3 7.0 %fusion.2 = bf16[1,256,7168]{2,1,0:T(8,128)(2,1)} fusion(bf16[480,256]{1,0:T(8,128)(2,1)S(1)} %get-tuple-element.12, bf16[480,7168]{1,0:T(8,128)(2,1)} %reshape.37), kind=kOutput, calls=%fused_computation.7 | convolution fusion | flops 1763442688 | bytes 10797056 | tf_op jit(solution)/shard_map/dot_general | solution.py:19
  254.4 0.0 slice-done
  254.4 0.0 slice-done.1
  254.4 4.0 %fusion.1 = bf16[1,7168,256]{2,1,0:T(8,128)(2,1)} fusion(bf16[480,7168]{1,0:T(8,128)(2,1)S(1)} %bitcast.46, bf16[480,256]{1,0:T(8,128)(2,1)S(1)} %get-tuple-element.13), kind=kOutput, calls=%fused_computation.6 | convolution fusion | flops 1763442688 | bytes 10797056 | tf_op jit(solution)/shard_map/dot_general | solution.py:19
  258.4 4.0 %fusion = bf16[1,7168,256]{2,1,0:T(8,128)(2,1)} fusion(bf16[480,7168]{1,0:T(8,128)(2,1)S(1)} %bitcast.46, bf16[480,256]{1,0:T(8,128)(2,1)S(1)} %get-tuple-element.14), kind=kOutput, calls=%fused_computation.5 | convolution fusion | flops 1763442688 | bytes 10797056 | tf_op jit(solution)/shard_map/dot_general | solution.py:19
  262.4 0.0 reduce-scatter.3.cloned.1.call-done
  262.4 31.6 %reduce-scatter.5.cloned.1.call-done = bf16[1,60,7168]{2,1,0:T(8,128)(2,1)} async-done(((bf16[8,60,7168]{2,1,0:T(8,128)(2,1)}), bf16[1,60,7168]{2,1,0:T(8,128)(2,1)}) %reduce-scatter.5.cloned.1.call-update) | async-done | bytes 860176 | tf_op jit(solution)/shard_map/reduce_scatter | solution.py:70
  (2 shorter events, 0.0 us)
Async XLA Ops:
  7.2 53.4 %all-gather.3.cloned.1.call-start = ((), (), s32[]{:S(2)}) async-start(), calls=%async_computation.5 | async-start | bytes 8257536 | tf_op jit(solution)/shard_map/all_gather | solution.py:58
  11.6 250.9 %reduce-scatter.3.cloned.1.call-start = ((), (), s32[]{:S(2)}) async-start(), calls=%async_computation.3 | async-start | bytes 8257536 | tf_op jit(solution)/shard_map/reduce_scatter | solution.py:67
  67.5 6.1 %copy-start = (bf16[480,7168]{1,0:T(8,128)(2,1)S(1)}, bf16[480,7168]{1,0:T(8,128)(2,1)}, u32[]{:S(2)}) copy-start(bf16[480,7168]{1,0:T(8,128)(2,1)} %reshape.40) | copy-start | bytes 20643844
  67.5 7.0 %copy-start.1 = (bf16[1,7168,256]{2,1,0:T(8,128)(2,1)S(1)}, bf16[1,7168,256]{2,1,0:T(8,128)(2,1)}, u32[]{:S(2)}) copy-start(bf16[1,7168,256]{2,1,0:T(8,128)(2,1)} %param.10) | copy-start | bytes 11010052
  74.5 2.0 copy-start.3
  88.2 1.2 copy-start.5
  88.2 205.8 %reduce-scatter.5.cloned.1.call-start = ((), (), s32[]{:S(2)}) async-start(), calls=%async_computation.4 | async-start | bytes 8257536 | tf_op jit(solution)/shard_map/reduce_scatter | solution.py:70
  217.6 6.2 %copy-start.4 = (bf16[1,7168,256]{2,1,0:T(8,128)(2,1)S(1)}, bf16[1,7168,256]{2,1,0:T(8,128)(2,1)}, u32[]{:S(2)}) copy-start(bf16[1,7168,256]{2,1,0:T(8,128)(2,1)} %param.9) | copy-start | bytes 11010052
  223.8 7.0 %copy-start.2 = (bf16[1,7168,256]{2,1,0:T(8,128)(2,1)S(1)}, bf16[1,7168,256]{2,1,0:T(8,128)(2,1)}, u32[]{:S(2)}) copy-start(bf16[1,7168,256]{2,1,0:T(8,128)(2,1)} %param.10) | copy-start | bytes 11010052
  247.3 7.1 %slice-start = ((s8[6881280]{0:T(1024)(128)(4,1)}), s8[2686976]{0:T(1024)(128)(4,1)S(1)}, s32[]{:S(2)}) async-start(s8[6881280]{0:T(1024)(128)(4,1)} %bitcast.45), calls=%async_computation.6 | async-start | bytes 5373952
  247.3 7.1 %slice-start.1 = ((s8[6881280]{0:T(1024)(128)(4,1)}), s8[4194304]{0:T(1024)(128)(4,1)S(1)}, s32[]{:S(2)}) async-start(s8[6881280]{0:T(1024)(128)(4,1)} %bitcast.45), calls=%async_computation.7 | async-start | bytes 8388608
Sparse Core Ops, SparseCore 0:
  11.7 48.8 all-gather.2
  88.3 122.8 reduce-scatter.2
  247.4 46.5 reduce-scatter.4
